TPU v7x, 512 devices: a whole 4x8x8 slice. The times are simulated.
512 devices in a mesh: req: 64 (over z, x, core), voc: 8 (over y).
Axes of the slice: x: 4, y: 8, z: 8, core: 2. Of those that a mesh axis runs over, the one named last changes fastest.
Arguments:
- hidden: bfloat16 [65536, 1600], P(('req', 'voc')), may hold values from -60 to 60
- norm_gain: float32 [1600], replicated, may hold values from 0.25 to 1.75
- unembed: bfloat16 [16384, 1600], P(('req', 'voc')), may hold values from -2 to 2
- targets: int32 [65536], P(('req', 'voc')), may hold values from 0 to 16383
- live: int32 [65536], P(('req', 'voc')), may hold values from 0 to 1, as said below
Outputs:
- logprob: float32 [65536], P(('req', 'voc'))
- entropy: float32 [65536], P(('req', 'voc'))
Inputs may be any that keep to these rules, and one draw needn't show every extreme that they name: Within each aligned block of 1024 slots (one owner's) the live slots form a prefix of 128 to 1024 slots, and in every draw at least one block is wholly live.
All inputs are finite; a program needn't handle non-finite values.
Results may differ from a plain program's by a relative error of at most 0.0067.
Values may be sent and summed in bfloat16 or wider, within the bound.
No kernel may reach another device: no remote copies, remote signals or barrier semaphores. Data moves between devices by JAX's collectives and lax.ppermute only.
A program may use at most 64 MiB of HBM per device.

v0:
```python
import jax
import jax.numpy as jnp
from jax import lax
from jax.sharding import Mesh, PartitionSpec as P

FLAT = ("z", "x", "c", "y")


def combine_stats(first, second):
    top = jnp.maximum(first[0], second[0])
    scale_one = jnp.exp(first[0] - top)
    scale_two = jnp.exp(second[0] - top)
    total = first[1] * scale_one + second[1] * scale_two
    spread = scale_one * (first[2] + (first[0] - top) * first[1]) + scale_two * (
        second[2] + (second[0] - top) * second[1]
    )
    return (top, total, spread, first[3] + second[3])


def shift(value, axis, size, step):
    return lax.ppermute(value, axis, [(i, (i + step) % size) for i in range(size)])


def chunk_stats(normed, piece, ids, wanted):
    logits = lax.dot_general(
        normed, piece, (((1,), (1,)), ((), ())), preferred_element_type=jnp.float32
    )
    chosen = jnp.sum(jnp.where(ids[None, :] == wanted[:, None], logits, 0.0), axis=1)
    fold_top = jnp.max(logits, axis=1)
    shifted = logits - fold_top[:, None]
    weights = jnp.exp(shifted)
    return (fold_top, jnp.sum(weights, axis=1), jnp.sum(weights * shifted, axis=1), chosen)


def on_device(hidden, norm_gain, unembed, targets, live):
    ny = lax.axis_size("y")
    nc = lax.axis_size("c")
    y = lax.axis_index("y")
    c = lax.axis_index("c")
    mine = hidden.shape[0]
    width = unembed.shape[0]
    wide = hidden.astype(jnp.float32)
    normed = (
        wide * lax.rsqrt(jnp.mean(wide * wide, axis=1, keepdims=True) + 1e-06) * norm_gain
    ).astype(jnp.bfloat16)
    blocks = [None] * ny
    blocks[0] = (normed, targets)
    fwd = ny // 2
    cur = (normed, targets)
    for d in range(1, fwd + 1):
        cur = shift(cur, "y", ny, 1)
        blocks[ny - d] = cur
    cur = (normed, targets)
    for d in range(1, ny - fwd):
        cur = shift(cur, "y", ny, -1)
        blocks[d] = cur
    rows = jnp.concatenate([b[0] for b in blocks], axis=0)
    wanted = jnp.concatenate([b[1] for b in blocks], axis=0)
    half = lax.all_gather(unembed, ("z", "x"), axis=0, tiled=True)
    other = shift(half, "c", nc, 1)

    def ids_of(core):
        local = jnp.arange(half.shape[0], dtype=jnp.int32)
        return (local // width * (nc * ny) + core * ny + y) * width + local % width

    count = rows.shape[0]
    zeros = jnp.zeros((count,), jnp.float32)
    stats = (jnp.full((count,), -1e30, jnp.float32), zeros, zeros, zeros)
    step = min(512, half.shape[0])
    for table, core in ((half, c), (other, (c + 1) % nc)):
        ids = ids_of(core)
        for first in range(0, table.shape[0], step):
            stats = combine_stats(
                stats,
                chunk_stats(rows, table[first : first + step], ids[first : first + step], wanted),
            )
    packed = jnp.stack(stats).reshape(4, ny, mine)
    merged = tuple(packed[:, 0])
    for d in range(1, ny):
        got = shift(packed[:, d], "y", ny, d)
        merged = combine_stats(merged, tuple(got))
    top, total, spread, picked = merged
    mask = live.astype(jnp.float32)
    logprob = (picked - top - jnp.log(total)) * mask
    entropy = (jnp.log(total) - spread / total) * mask
    return (logprob, entropy)


def solution(mesh):
    nz, nx, nc = (8, 4, 2)
    ny = mesh.devices.shape[1]
    req = mesh.devices.shape[0]
    nz = req // (nx * nc)
    flat = Mesh(mesh.devices.reshape(nz, nx, nc, ny), FLAT)
    return jax.shard_map(
        on_device,
        mesh=flat,
        in_specs=(P(FLAT, None), P(), P(FLAT, None), P(FLAT), P(FLAT)),
        out_specs=(P(FLAT), P(FLAT)),
        check_vma=False,
    )
```

profile of v0, /device:TPU:56, one launch (start us, length us, event | category | flops | bytes accessed | tf_op | source)
XLA Modules:
  0.0 202.6 jit_solution(11467726991118370099)
XLA Ops:
  7.2 0.0 all-gather.2.cloned.1.call-start
  7.2 0.7 all-gather.2.cloned.1.call-update
  7.9 1.2 fusion.12
  9.1 2.2 %constant_dynamic-update-slice_fusion.8 = (bf16[1024,1600]{0,1:T(8,128)(2,1)}, bf16[128,1600]{0,1:T(8,128)(2,1)}) fusion(f32[1600]{0:T(1024)} %param.6, f32[128]{0:T(128)S(1)} %add_rsqrt_fusion, bf16[128,1600]{0,1:T(8,128)(2,1)} %param.5), kind=kLoop, calls=%fused_computation.37 | loop fusion | flops 819199 | bytes 1235712
  11.4 3.2 %collective-permute-start.7 = (bf16[128,1600]{0,1:T(8,128)(2,1)}, bf16[128,1600]{0,1:T(8,128)(2,1)}, u32[]{:S(2)}, u32[]{:S(2)}) collective-permute-start(bf16[128,1600]{0,1:T(8,128)(2,1)} %get-tuple-element.18), channel_id=1, source_target_pairs={{0,7},{1,0},{2,1},{3,2},{4,3},{5,4},{6,5},{7,6},{8,15},{9,8},{10,9... | collective-permute-start | bytes 1228808 | tf_op jit(solution)/shard_map/ppermute | solution.py:21
  14.6 5.7 %collective-permute-start.10 = (bf16[128,1600]{0,1:T(8,128)(2,1)}, bf16[128,1600]{0,1:T(8,128)(2,1)}, u32[]{:S(2)}, u32[]{:S(2)}) collective-permute-start(bf16[128,1600]{0,1:T(8,128)(2,1)} %get-tuple-element.18), channel_id=1, source_target_pairs={{0,1},{1,2},{2,3},{3,4},{4,5},{5,6},{6,7},{7,0},{8,9},{9,10},{10,1... | collective-permute-start | bytes 1228808 | tf_op jit(solution)/shard_map/ppermute | solution.py:21
  20.3 1.9 collective-permute-start
  22.3 5.1 %collective-permute-start.3 = (s32[128]{0:T(128)}, s32[128]{0:T(128)S(1)}, u32[]{:S(2)}, u32[]{:S(2)}) collective-permute-start(s32[128]{0:T(128)} %param.8), channel_id=1, source_target_pairs={{0,1},{1,2},{2,3},{3,4},{4,5},{5,6},{6,7},{7,0},{8,9},{9,10},{10,1... | collective-permute-start | bytes 1544 | tf_op jit(solution)/shard_map/ppermute | solution.py:21
  27.5 0.7 constant_dynamic-update-slice_fusion
  28.2 0.0 collective-permute-done
  28.2 1.9 collective-permute-start.1
  30.1 0.0 collective-permute-done.3
  30.1 5.1 %collective-permute-start.4 = (s32[128]{0:T(128)S(1)}, s32[128]{0:T(128)S(1)}, u32[]{:S(2)}, u32[]{:S(2)}) collective-permute-start(s32[128]{0:T(128)S(1)} %collective-permute-done.3), channel_id=1, source_target_pairs={{0,1},{1,2},{2,3},{3,4},{4,5},{5,6},{6,7},{7,0},{8,9},{9,10},{10,1... | collective-permute-start | bytes 1544 | tf_op jit(solution)/shard_map/ppermute | solution.py:21
  35.2 0.0 collective-permute-done.1
  35.3 1.9 collective-permute-start.2
  37.2 0.0 collective-permute-done.4
  37.2 5.1 %collective-permute-start.5 = (s32[128]{0:T(128)S(1)}, s32[128]{0:T(128)S(1)}, u32[]{:S(2)}, u32[]{:S(2)}) collective-permute-start(s32[128]{0:T(128)S(1)} %collective-permute-done.4), channel_id=1, source_target_pairs={{0,1},{1,2},{2,3},{3,4},{4,5},{5,6},{6,7},{7,0},{8,9},{9,10},{10,1... | collective-permute-start | bytes 1544 | tf_op jit(solution)/shard_map/ppermute | solution.py:21
  42.3 0.0 collective-permute-done.10
  42.3 1.9 collective-permute-start.11
  44.3 0.0 collective-permute-done.5
  44.3 4.7 %collective-permute-start.6 = (s32[128]{0:T(128)S(1)}, s32[128]{0:T(128)S(1)}, u32[]{:S(2)}, u32[]{:S(2)}) collective-permute-start(s32[128]{0:T(128)S(1)} %collective-permute-done.5), channel_id=1, source_target_pairs={{0,1},{1,2},{2,3},{3,4},{4,5},{5,6},{6,7},{7,0},{8,9},{9,10},{10,1... | collective-permute-start | bytes 1544 | tf_op jit(solution)/shard_map/ppermute | solution.py:21
  49.0 52.7 %all-gather.2.cloned.1.call-done = bf16[1024,1600]{1,0:T(8,128)(2,1)} async-done(((bf16[32,1600]{1,0:T(8,128)(2,1)}), bf16[1024,1600]{1,0:T(8,128)(2,1)}) %all-gather.2.cloned.1.call-update) | async-done | bytes 3276816 | tf_op jit(solution)/shard_map/all_gather | solution.py:59
  101.7 4.3 %copy.9 = bf16[1024,1600]{0,1:T(8,128)(2,1)S(1)} copy(bf16[1024,1600]{1,0:T(8,128)(2,1)} %all-gather.2.cloned.1.call-done) | data formatting | bytes 6553600 | tf_op jit(solution)/shard_map/all_gather | solution.py:59
  106.0 2.2 %collective-permute-start.14 = (bf16[1024,1600]{0,1:T(8,128)(2,1)S(1)}, bf16[1024,1600]{0,1:T(8,128)(2,1)S(1)}, u32[]{:S(2)}, u32[]{:S(2)}) collective-permute-start(bf16[1024,1600]{0,1:T(8,128)(2,1)S(1)} %copy.9), channel_id=1, source_target_pairs={{0,8},{8,0},{1,9},{9,1},{2,10},{10,2},{3,11},{11,3},{4,12},{12,4},... | collective-permute-start | bytes 9830408 | tf_op jit(solution)/shard_map/ppermute | solution.py:21
  108.2 0.0 collective-permute-done.2
  108.2 0.0 collective-permute-done.7
  108.2 3.3 %collective-permute-start.8 = (bf16[128,1600]{0,1:T(8,128)(2,1)}, bf16[128,1600]{0,1:T(8,128)(2,1)S(1)}, u32[]{:S(2)}, u32[]{:S(2)}) collective-permute-start(bf16[128,1600]{0,1:T(8,128)(2,1)} %collective-permute-done.7), channel_id=1, source_target_pairs={{0,7},{1,0},{2,1},{3,2},{4,3},{5,4},{6,5},{7,6},{8,15},{9,8},{10,9... | collective-permute-start | bytes 1228808 | tf_op jit(solution)/shard_map/ppermute | solution.py:21
  111.6 0.0 collective-permute-done.6
  111.6 0.0 collective-permute-done.11
  111.6 3.7 %collective-permute-start.12 = (bf16[128,1600]{0,1:T(8,128)(2,1)}, bf16[128,1600]{0,1:T(8,128)(2,1)S(1)}, u32[]{:S(2)}, u32[]{:S(2)}) collective-permute-start(bf16[128,1600]{0,1:T(8,128)(2,1)} %collective-permute-done.11), channel_id=1, source_target_pairs={{0,1},{1,2},{2,3},{3,4},{4,5},{5,6},{6,7},{7,0},{8,9},{9,10},{10,1... | collective-permute-start | bytes 1228808 | tf_op jit(solution)/shard_map/ppermute | solution.py:21
  115.3 8.0 %collective-permute-done.8 = bf16[128,1600]{0,1:T(8,128)(2,1)S(1)} collective-permute-done((bf16[128,1600]{0,1:T(8,128)(2,1)}, bf16[128,1600]{0,1:T(8,128)(2,1)S(1)}, u32[]{:S(2)}, u32[]{:S(2)}) %collective-permute-start.8) | collective-permute-done | bytes 409632 | tf_op jit(solution)/shard_map/ppermute | solution.py:21
  123.4 2.1 %collective-permute-start.9 = (bf16[128,1600]{0,1:T(8,128)(2,1)S(1)}, bf16[128,1600]{0,1:T(8,128)(2,1)S(1)}, u32[]{:S(2)}, u32[]{:S(2)}) collective-permute-start(bf16[128,1600]{0,1:T(8,128)(2,1)S(1)} %collective-permute-done.8), channel_id=1, source_target_pairs={{0,7},{1,0},{2,1},{3,2},{4,3},{5,4},{6,5},{7,6},{8,15},{9,8},{10,9... | collective-permute-start | bytes 1228808 | tf_op jit(solution)/shard_map/ppermute | solution.py:21
  125.5 1.8 constant_dynamic-update-slice_fusion.7
  127.4 0.0 collective-permute-done.12
  127.4 4.9 %collective-permute-start.13 = (bf16[128,1600]{0,1:T(8,128)(2,1)S(1)}, bf16[128,1600]{0,1:T(8,128)(2,1)S(1)}, u32[]{:S(2)}, u32[]{:S(2)}) collective-permute-start(bf16[128,1600]{0,1:T(8,128)(2,1)S(1)} %collective-permute-done.12), channel_id=1, source_target_pairs={{0,1},{1,2},{2,3},{3,4},{4,5},{5,6},{6,7},{7,0},{8,9},{9,10},{10,1... | collective-permute-start | bytes 1228808 | tf_op jit(solution)/shard_map/ppermute | solution.py:21
  132.3 0.8 constant_dynamic-update-slice_fusion.6
  133.1 4.5 %collective-permute-done.9 = bf16[128,1600]{0,1:T(8,128)(2,1)S(1)} collective-permute-done((bf16[128,1600]{0,1:T(8,128)(2,1)S(1)}, bf16[128,1600]{0,1:T(8,128)(2,1)S(1)}, u32[]{:S(2)}, u32[]{:S(2)}) %collective-permute-start.9) | collective-permute-done | bytes 409632 | tf_op jit(solution)/shard_map/ppermute | solution.py:21
  137.6 0.8 constant_dynamic-update-slice_fusion.5
  138.4 2.2 %collective-permute-done.13 = bf16[128,1600]{0,1:T(8,128)(2,1)S(1)} collective-permute-done((bf16[128,1600]{0,1:T(8,128)(2,1)S(1)}, bf16[128,1600]{0,1:T(8,128)(2,1)S(1)}, u32[]{:S(2)}, u32[]{:S(2)}) %collective-permute-start.13) | collective-permute-done | bytes 409632 | tf_op jit(solution)/shard_map/ppermute | solution.py:21
  140.6 0.8 constant_dynamic-update-slice_fusion.4
  141.4 0.8 constant_dynamic-update-slice_fusion.3
  142.2 1.8 constant_dynamic-update-slice_fusion.2
  144.0 1.8 constant_dynamic-update-slice_fusion.1
  145.9 4.2 %fusion.87 = (f32[1024]{0:T(1024)S(1)}, f32[1024,512]{0,1:T(8,128)S(1)}) fusion(bf16[1024,1600]{0,1:T(8,128)(2,1)} %constant_dynamic-update-slice_fusion.1, bf16[1024,1600]{1,0:T(8,128)(2,1)S(1)} %copy-done), kind=kOutput, calls=%fused_computation.198 | convolution fusion | flops 1678244864 | bytes 7081984 | tf_op jit(solution)/shard_map/dot_general | solution.py:25
  150.1 2.1 %fusion.90 = (f32[1024]{0:T(1024)S(1)}, f32[1024,512]{0,1:T(8,128)S(1)}) fusion(bf16[1024,1600]{0,1:T(8,128)(2,1)S(1)} %copy-done.1, bf16[1024,1600]{1,0:T(8,128)(2,1)S(1)} %copy-done), kind=kOutput, calls=%fused_computation.201 | convolution fusion | flops 1678244864 | bytes 7081984 | tf_op jit(solution)/shard_map/dot_general | solution.py:25
  152.1 0.0 collective-permute-done.14
  152.2 2.1 %fusion.88 = (f32[1024]{0:T(1024)S(1)}, f32[1024,512]{0,1:T(8,128)S(1)}) fusion(bf16[1024,1600]{0,1:T(8,128)(2,1)S(1)} %copy-done.1, bf16[1024,1600]{0,1:T(8,128)(2,1)S(1)} %collective-permute-done.14), kind=kOutput, calls=%fused_computation.199 | convolution fusion | flops 1678244864 | bytes 7016448 | tf_op jit(solution)/shard_map/dot_general | solution.py:25
  154.3 2.2 %fusion.89 = (f32[1024]{0:T(1024)S(1)}, f32[1024,512]{0,1:T(8,128)S(1)}) fusion(bf16[1024,1600]{0,1:T(8,128)(2,1)S(1)} %copy-done.1, bf16[1024,1600]{0,1:T(8,128)(2,1)S(1)} %collective-permute-done.14), kind=kOutput, calls=%fused_computation.200 | convolution fusion | flops 1678244864 | bytes 7016448 | tf_op jit(solution)/shard_map/dot_general | solution.py:25
  156.5 0.0 copy-start.2
  156.5 3.9 %exponential_reduce_fusion.2 = (f32[1024]{0:T(1024)S(1)}, f32[1024]{0:T(1024)S(1)}, f32[1024]{0:T(1024)S(1)}, f32[1024]{0:T(1024)S(1)}, f32[1024]{0:T(1024)S(1)}...) fusion(f32[1024,512]{0,1:T(8,128)S(1)} %get-tuple-element.43, ...), kind=kLoop, calls=%fused_computation.5 | loop fusion | flops 14667776 | bytes 8466432 | tf_op jit(solution)/shard_map/reduce_sum | solution.py:32
  160.5 5.6 %collective-permute-start.15 = (f32[4,128]{1,0:T(4,128)S(1)}, f32[4,128]{1,0:T(4,128)S(1)}, u32[]{:S(2)}, u32[]{:S(2)}) collective-permute-start(f32[4,128]{1,0:T(4,128)S(1)} %bitcast.594), channel_id=1, source_target_pairs={{0,1},{1,2},{2,3},{3,4},{4,5},{5,6},{6,7},{7,0},{8,9},{9,10},{10,1... | collective-permute-start | bytes 6152 | tf_op jit(solution)/shard_map/ppermute | solution.py:21
  166.1 5.1 %collective-permute-start.18 = (f32[4,128]{1,0:T(4,128)S(1)}, f32[4,128]{1,0:T(4,128)S(1)}, u32[]{:S(2)}, u32[]{:S(2)}) collective-permute-start(f32[4,128]{1,0:T(4,128)S(1)} %bitcast.593), channel_id=1, source_target_pairs={{0,4},{1,5},{2,6},{3,7},{4,0},{5,1},{6,2},{7,3},{8,12},{9,13},{10,... | collective-permute-start | bytes 6152 | tf_op jit(solution)/shard_map/ppermute | solution.py:21
  171.2 2.0 collective-permute-start.19
  173.2 2.9 %collective-permute-start.20 = (f32[4,128]{1,0:T(4,128)S(1)}, f32[4,128]{1,0:T(4,128)S(1)}, u32[]{:S(2)}, u32[]{:S(2)}) collective-permute-start(f32[4,128]{1,0:T(4,128)S(1)} %bitcast.591), channel_id=1, source_target_pairs={{0,6},{1,7},{2,0},{3,1},{4,2},{5,3},{6,4},{7,5},{8,14},{9,15},{10,... | collective-permute-start | bytes 6152 | tf_op jit(solution)/shard_map/ppermute | solution.py:21
  176.1 5.0 %collective-permute-start.16 = (f32[4,128]{1,0:T(4,128)S(1)}, f32[4,128]{1,0:T(4,128)S(1)}, u32[]{:S(2)}, u32[]{:S(2)}) collective-permute-start(f32[4,128]{1,0:T(4,128)S(1)} %bitcast.597), channel_id=1, source_target_pairs={{0,2},{1,3},{2,4},{3,5},{4,6},{5,7},{6,0},{7,1},{8,10},{9,11},{10,... | collective-permute-start | bytes 6152 | tf_op jit(solution)/shard_map/ppermute | solution.py:21
  181.2 0.0 collective-permute-done.15
  181.2 6.8 %collective-permute-start.17 = (f32[4,128]{1,0:T(4,128)S(1)}, f32[4,128]{1,0:T(4,128)S(1)}, u32[]{:S(2)}, u32[]{:S(2)}) collective-permute-start(f32[4,128]{1,0:T(4,128)S(1)} %bitcast.596), channel_id=1, source_target_pairs={{0,3},{1,4},{2,5},{3,6},{4,7},{5,0},{6,1},{7,2},{8,11},{9,12},{10,... | collective-permute-start | bytes 6152 | tf_op jit(solution)/shard_map/ppermute | solution.py:21
  188.0 0.0 collective-permute-done.18
  188.0 1.9 collective-permute-start.21
  190.0 0.0 collective-permute-done.20
  190.0 0.0 collective-permute-done.16
  190.0 4.7 %collective-permute-done.21 = f32[4,128]{1,0:T(4,128)S(1)} collective-permute-done((f32[4,128]{1,0:T(4,128)S(1)}, f32[4,128]{1,0:T(4,128)S(1)}, u32[]{:S(2)}, u32[]{:S(2)}) %collective-permute-start.21) | collective-permute-done | bytes 2080 | tf_op jit(solution)/shard_map/ppermute | solution.py:21
  194.7 0.5 subtract_multiply_fusion
  195.3 0.5 fusion.82
  (23 shorter events, 0.1 us)
Async XLA Ops:
  7.2 94.5 %all-gather.2.cloned.1.call-start = ((), (), s32[]{:S(2)}) async-start(), calls=%async_computation | async-start | bytes 3514368 | tf_op jit(solution)/shard_map/all_gather | solution.py:59
  11.4 96.8 %collective-permute-start.7 = (bf16[128,1600]{0,1:T(8,128)(2,1)}, bf16[128,1600]{0,1:T(8,128)(2,1)}, u32[]{:S(2)}, u32[]{:S(2)}) collective-permute-start(bf16[128,1600]{0,1:T(8,128)(2,1)} %get-tuple-element.18), channel_id=1, source_target_pairs={{0,7},{1,0},{2,1},{3,2},{4,3},{5,4},{6,5},{7,6},{8,15},{9,8},{10,9... | collective-permute-start | bytes 1228808 | tf_op jit(solution)/shard_map/ppermute | solution.py:21
  14.6 27.7 %collective-permute-start.10 = (bf16[128,1600]{0,1:T(8,128)(2,1)}, bf16[128,1600]{0,1:T(8,128)(2,1)}, u32[]{:S(2)}, u32[]{:S(2)}) collective-permute-start(bf16[128,1600]{0,1:T(8,128)(2,1)} %get-tuple-element.18), channel_id=1, source_target_pairs={{0,1},{1,2},{2,3},{3,4},{4,5},{5,6},{6,7},{7,0},{8,9},{9,10},{10,1... | collective-permute-start | bytes 1228808 | tf_op jit(solution)/shard_map/ppermute | solution.py:21
  20.3 7.8 %collective-permute-start = (s32[128]{0:T(128)}, s32[128]{0:T(128)S(1)}, u32[]{:S(2)}, u32[]{:S(2)}) collective-permute-start(s32[128]{0:T(128)} %param.8), channel_id=1, source_target_pairs={{0,7},{1,0},{2,1},{3,2},{4,3},{5,4},{6,5},{7,6},{8,15},{9,8},{10,9... | collective-permute-start | bytes 1544 | tf_op jit(solution)/shard_map/ppermute | solution.py:21
  22.3 7.8 %collective-permute-start.3 = (s32[128]{0:T(128)}, s32[128]{0:T(128)S(1)}, u32[]{:S(2)}, u32[]{:S(2)}) collective-permute-start(s32[128]{0:T(128)} %param.8), channel_id=1, source_target_pairs={{0,1},{1,2},{2,3},{3,4},{4,5},{5,6},{6,7},{7,0},{8,9},{9,10},{10,1... | collective-permute-start | bytes 1544 | tf_op jit(solution)/shard_map/ppermute | solution.py:21
  28.2 7.1 %collective-permute-start.1 = (s32[128]{0:T(128)S(1)}, s32[128]{0:T(128)S(1)}, u32[]{:S(2)}, u32[]{:S(2)}) collective-permute-start(s32[128]{0:T(128)S(1)} %collective-permute-done), channel_id=1, source_target_pairs={{0,7},{1,0},{2,1},{3,2},{4,3},{5,4},{6,5},{7,6},{8,15},{9,8},{10,9... | collective-permute-start | bytes 1544 | tf_op jit(solution)/shard_map/ppermute | solution.py:21
  30.1 7.1 %collective-permute-start.4 = (s32[128]{0:T(128)S(1)}, s32[128]{0:T(128)S(1)}, u32[]{:S(2)}, u32[]{:S(2)}) collective-permute-start(s32[128]{0:T(128)S(1)} %collective-permute-done.3), channel_id=1, source_target_pairs={{0,1},{1,2},{2,3},{3,4},{4,5},{5,6},{6,7},{7,0},{8,9},{9,10},{10,1... | collective-permute-start | bytes 1544 | tf_op jit(solution)/shard_map/ppermute | solution.py:21
  35.3 72.9 %collective-permute-start.2 = (s32[128]{0:T(128)S(1)}, s32[128]{0:T(128)S(1)}, u32[]{:S(2)}, u32[]{:S(2)}) collective-permute-start(s32[128]{0:T(128)S(1)} %collective-permute-done.1), channel_id=1, source_target_pairs={{0,7},{1,0},{2,1},{3,2},{4,3},{5,4},{6,5},{7,6},{8,15},{9,8},{10,9... | collective-permute-start | bytes 1544 | tf_op jit(solution)/shard_map/ppermute | solution.py:21
  37.2 7.1 %collective-permute-start.5 = (s32[128]{0:T(128)S(1)}, s32[128]{0:T(128)S(1)}, u32[]{:S(2)}, u32[]{:S(2)}) collective-permute-start(s32[128]{0:T(128)S(1)} %collective-permute-done.4), channel_id=1, source_target_pairs={{0,1},{1,2},{2,3},{3,4},{4,5},{5,6},{6,7},{7,0},{8,9},{9,10},{10,1... | collective-permute-start | bytes 1544 | tf_op jit(solution)/shard_map/ppermute | solution.py:21
  42.3 69.3 %collective-permute-start.11 = (bf16[128,1600]{0,1:T(8,128)(2,1)}, bf16[128,1600]{0,1:T(8,128)(2,1)}, u32[]{:S(2)}, u32[]{:S(2)}) collective-permute-start(bf16[128,1600]{0,1:T(8,128)(2,1)} %collective-permute-done.10), channel_id=1, source_target_pairs={{0,1},{1,2},{2,3},{3,4},{4,5},{5,6},{6,7},{7,0},{8,9},{9,10},{10,1... | collective-permute-start | bytes 1228808 | tf_op jit(solution)/shard_map/ppermute | solution.py:21
  44.3 67.3 %collective-permute-start.6 = (s32[128]{0:T(128)S(1)}, s32[128]{0:T(128)S(1)}, u32[]{:S(2)}, u32[]{:S(2)}) collective-permute-start(s32[128]{0:T(128)S(1)} %collective-permute-done.5), channel_id=1, source_target_pairs={{0,1},{1,2},{2,3},{3,4},{4,5},{5,6},{6,7},{7,0},{8,9},{9,10},{10,1... | collective-permute-start | bytes 1544 | tf_op jit(solution)/shard_map/ppermute | solution.py:21
  106.0 39.9 %copy-start = (bf16[1024,1600]{1,0:T(8,128)(2,1)S(1)}, bf16[1024,1600]{1,0:T(8,128)(2,1)}, u32[]{:S(2)}) copy-start(bf16[1024,1600]{1,0:T(8,128)(2,1)} %all-gather.2.cloned.1.call-done) | copy-start | bytes 9830404
  106.0 46.2 %collective-permute-start.14 = (bf16[1024,1600]{0,1:T(8,128)(2,1)S(1)}, bf16[1024,1600]{0,1:T(8,128)(2,1)S(1)}, u32[]{:S(2)}, u32[]{:S(2)}) collective-permute-start(bf16[1024,1600]{0,1:T(8,128)(2,1)S(1)} %copy.9), channel_id=1, source_target_pairs={{0,8},{8,0},{1,9},{9,1},{2,10},{10,2},{3,11},{11,3},{4,12},{12,4},... | collective-permute-start | bytes 9830408 | tf_op jit(solution)/shard_map/ppermute | solution.py:21
  108.2 15.2 %collective-permute-start.8 = (bf16[128,1600]{0,1:T(8,128)(2,1)}, bf16[128,1600]{0,1:T(8,128)(2,1)S(1)}, u32[]{:S(2)}, u32[]{:S(2)}) collective-permute-start(bf16[128,1600]{0,1:T(8,128)(2,1)} %collective-permute-done.7), channel_id=1, source_target_pairs={{0,7},{1,0},{2,1},{3,2},{4,3},{5,4},{6,5},{7,6},{8,15},{9,8},{10,9... | collective-permute-start | bytes 1228808 | tf_op jit(solution)/shard_map/ppermute | solution.py:21
  111.6 15.8 %collective-permute-start.12 = (bf16[128,1600]{0,1:T(8,128)(2,1)}, bf16[128,1600]{0,1:T(8,128)(2,1)S(1)}, u32[]{:S(2)}, u32[]{:S(2)}) collective-permute-start(bf16[128,1600]{0,1:T(8,128)(2,1)} %collective-permute-done.11), channel_id=1, source_target_pairs={{0,1},{1,2},{2,3},{3,4},{4,5},{5,6},{6,7},{7,0},{8,9},{9,10},{10,1... | collective-permute-start | bytes 1228808 | tf_op jit(solution)/shard_map/ppermute | solution.py:21
  123.4 14.2 %collective-permute-start.9 = (bf16[128,1600]{0,1:T(8,128)(2,1)S(1)}, bf16[128,1600]{0,1:T(8,128)(2,1)S(1)}, u32[]{:S(2)}, u32[]{:S(2)}) collective-permute-start(bf16[128,1600]{0,1:T(8,128)(2,1)S(1)} %collective-permute-done.8), channel_id=1, source_target_pairs={{0,7},{1,0},{2,1},{3,2},{4,3},{5,4},{6,5},{7,6},{8,15},{9,8},{10,9... | collective-permute-start | bytes 1228808 | tf_op jit(solution)/shard_map/ppermute | solution.py:21
  127.4 13.2 %collective-permute-start.13 = (bf16[128,1600]{0,1:T(8,128)(2,1)S(1)}, bf16[128,1600]{0,1:T(8,128)(2,1)S(1)}, u32[]{:S(2)}, u32[]{:S(2)}) collective-permute-start(bf16[128,1600]{0,1:T(8,128)(2,1)S(1)} %collective-permute-done.12), channel_id=1, source_target_pairs={{0,1},{1,2},{2,3},{3,4},{4,5},{5,6},{6,7},{7,0},{8,9},{9,10},{10,1... | collective-permute-start | bytes 1228808 | tf_op jit(solution)/shard_map/ppermute | solution.py:21
  145.9 4.2 %copy-start.1 = (bf16[1024,1600]{0,1:T(8,128)(2,1)S(1)}, bf16[1024,1600]{0,1:T(8,128)(2,1)}, u32[]{:S(2)}) copy-start(bf16[1024,1600]{0,1:T(8,128)(2,1)} %constant_dynamic-update-slice_fusion.1) | copy-start | bytes 9830404
  156.5 38.2 %copy-start.2 = (s32[128]{0:T(128)S(1)}, s32[128]{0:T(128)}, u32[]{:S(2)}) copy-start(s32[128]{0:T(128)} %param.9) | copy-start | bytes 1540
  160.5 20.7 %collective-permute-start.15 = (f32[4,128]{1,0:T(4,128)S(1)}, f32[4,128]{1,0:T(4,128)S(1)}, u32[]{:S(2)}, u32[]{:S(2)}) collective-permute-start(f32[4,128]{1,0:T(4,128)S(1)} %bitcast.594), channel_id=1, source_target_pairs={{0,1},{1,2},{2,3},{3,4},{4,5},{5,6},{6,7},{7,0},{8,9},{9,10},{10,1... | collective-permute-start | bytes 6152 | tf_op jit(solution)/shard_map/ppermute | solution.py:21
  166.1 21.9 %collective-permute-start.18 = (f32[4,128]{1,0:T(4,128)S(1)}, f32[4,128]{1,0:T(4,128)S(1)}, u32[]{:S(2)}, u32[]{:S(2)}) collective-permute-start(f32[4,128]{1,0:T(4,128)S(1)} %bitcast.593), channel_id=1, source_target_pairs={{0,4},{1,5},{2,6},{3,7},{4,0},{5,1},{6,2},{7,3},{8,12},{9,13},{10,... | collective-permute-start | bytes 6152 | tf_op jit(solution)/shard_map/ppermute | solution.py:21
  171.2 18.8 %collective-permute-start.19 = (f32[4,128]{1,0:T(4,128)S(1)}, f32[4,128]{1,0:T(4,128)S(1)}, u32[]{:S(2)}, u32[]{:S(2)}) collective-permute-start(f32[4,128]{1,0:T(4,128)S(1)} %bitcast.592), channel_id=1, source_target_pairs={{0,5},{1,6},{2,7},{3,0},{4,1},{5,2},{6,3},{7,4},{8,13},{9,14},{10,... | collective-permute-start | bytes 6152 | tf_op jit(solution)/shard_map/ppermute | solution.py:21
  173.2 16.8 %collective-permute-start.20 = (f32[4,128]{1,0:T(4,128)S(1)}, f32[4,128]{1,0:T(4,128)S(1)}, u32[]{:S(2)}, u32[]{:S(2)}) collective-permute-start(f32[4,128]{1,0:T(4,128)S(1)} %bitcast.591), channel_id=1, source_target_pairs={{0,6},{1,7},{2,0},{3,1},{4,2},{5,3},{6,4},{7,5},{8,14},{9,15},{10,... | collective-permute-start | bytes 6152 | tf_op jit(solution)/shard_map/ppermute | solution.py:21
  176.1 13.9 %collective-permute-start.16 = (f32[4,128]{1,0:T(4,128)S(1)}, f32[4,128]{1,0:T(4,128)S(1)}, u32[]{:S(2)}, u32[]{:S(2)}) collective-permute-start(f32[4,128]{1,0:T(4,128)S(1)} %bitcast.597), channel_id=1, source_target_pairs={{0,2},{1,3},{2,4},{3,5},{4,6},{5,7},{6,0},{7,1},{8,10},{9,11},{10,... | collective-permute-start | bytes 6152 | tf_op jit(solution)/shard_map/ppermute | solution.py:21
  181.2 8.8 %collective-permute-start.17 = (f32[4,128]{1,0:T(4,128)S(1)}, f32[4,128]{1,0:T(4,128)S(1)}, u32[]{:S(2)}, u32[]{:S(2)}) collective-permute-start(f32[4,128]{1,0:T(4,128)S(1)} %bitcast.596), channel_id=1, source_target_pairs={{0,3},{1,4},{2,5},{3,6},{4,7},{5,0},{6,1},{7,2},{8,11},{9,12},{10,... | collective-permute-start | bytes 6152 | tf_op jit(solution)/shard_map/ppermute | solution.py:21
  188.0 6.7 %collective-permute-start.21 = (f32[4,128]{1,0:T(4,128)S(1)}, f32[4,128]{1,0:T(4,128)S(1)}, u32[]{:S(2)}, u32[]{:S(2)}) collective-permute-start(f32[4,128]{1,0:T(4,128)S(1)} %bitcast.595), channel_id=1, source_target_pairs={{0,7},{1,0},{2,1},{3,2},{4,3},{5,4},{6,5},{7,6},{8,15},{9,8},{10,9... | collective-permute-start | bytes 6152 | tf_op jit(solution)/shard_map/ppermute | solution.py:21
Sparse Core Ops, SparseCore 0:
  11.2 90.4 all-gather.1
where the time goes:
time: 204 us; the launch traced here: 203 us
  starting transfers between devices  82.5 us (40%)
  waiting for transfers between devices  72.8 us (36%)
  between operations  14.5 us (7%)
  local copies, waits for them, and re-layouts  13.7 us (7%)
  matrix products  10.6 us (5%)
  other arithmetic  8.53 us (4%)
    ppermute x22, starting transfers between devices, shift(): lax.ppermute(value, axis, [(i, (i + step) % size) for i in range(size)])  82.4 us
    all_gather x1, waiting for transfers between devices, on_device(): half = lax.all_gather(unembed, ('z', 'x'), axis=0, tiled=True)  52.7 us
    ppermute x22, waiting for transfers between devices, shift(): lax.ppermute(value, axis, [(i, (i + step) % size) for i in range(size)])  19.5 us
    dot_general x4, matrix products, chunk_stats(): lax.dot_general(normed, piece, (((1,), (1,)), ((), ())), preferred_elemen...  10.6 us
    unnamed x19, local copies, waits for them, and re-layouts  7.66 us
    all_gather x1, local copies, waits for them, and re-layouts, on_device(): half = lax.all_gather(unembed, ('z', 'x'), axis=0, tiled=True)  4.26 us
  transfers between devices with their start and end apart: 23, of which 5 were waited for; matrix products, arithmetic and copies ran while one was open for 12% of the time, Pallas kernels for 0%

commit v1 on v0

--- a/solution.py
+++ b/solution.py
@@ -56,7 +56,9 @@
         blocks[d] = cur
     rows = jnp.concatenate([b[0] for b in blocks], axis=0)
     wanted = jnp.concatenate([b[1] for b in blocks], axis=0)
-    half = lax.all_gather(unembed, ("z", "x"), axis=0, tiled=True)
+    half = jnp.concatenate(
+        lax.all_to_all(jnp.stack([unembed] * lax.axis_size(("z", "x"))), ("z", "x"), 0, 0), axis=0
+    )
     other = shift(half, "c", nc, 1)
 
     def ids_of(core):

time: 204 us -> 173 us (0.85)
  waiting for transfers between devices: 72.8 us -> 45.1 us
  between operations: 14.5 us -> 1.13 us
  local copies, waits for them, and re-layouts: 13.7 us -> 20.2 us
  starting transfers between devices: 82.5 us -> 88.5 us
  matrix products: 10.6 us -> 8.53 us
    all_gather x1 -> x0, waiting for transfers between devices: 52.7 us -> none  [on_device(): half = lax.all_gather(unembed, ('z', 'x'), axis=0, tiled=True)]
    all_to_all x0 -> x1, waiting for transfers between devices: none -> 25.8 us  [on_device(): lax.all_to_all(jnp.stack([unembed] * lax.axis_size(('z', 'x'))), ('z', 'x...]
    all_to_all x0 -> x1, starting transfers between devices: none -> 13.3 us  [on_device(): lax.all_to_all(jnp.stack([unembed] * lax.axis_size(('z', 'x'))), ('z', 'x...]
    ppermute x22, starting transfers between devices: 82.4 us -> 75.2 us  [shift(): lax.ppermute(value, axis, [(i, (i + step) % size) for i in range(size)])]
    all_gather x1 -> x0, local copies, waits for them, and re-layouts: 4.26 us -> none  [on_device(): half = lax.all_gather(unembed, ('z', 'x'), axis=0, tiled=True)]
    unnamed x19 -> x21, local copies, waits for them, and re-layouts: 7.66 us -> 11.7 us
    reshape x0 -> x1, local copies, waits for them, and re-layouts: none -> 3.59 us  [on_device(): jnp.concatenate(lax.all_to_all(jnp.stack([unembed] * lax.axis_size(('z',...]
    another operation x0 -> x1, local copies, waits for them, and re-layouts: none -> 2.85 us  [on_device(): jnp.stack([unembed] * lax.axis_size(('z', 'x')))]
  transfers between devices with their start and end apart: 23 -> 23, of which waited for: 5 -> 6; matrix products, arithmetic and copies ran while one was open for 12% -> 14% of each run, Pallas kernels for 0% -> 0%
where the time goes in v1:
time: 173 us; the launch traced here: 172 us
  starting transfers between devices  88.5 us (51%)
  waiting for transfers between devices  45.1 us (26%)
  local copies, waits for them, and re-layouts  20.2 us (12%)
  matrix products  8.53 us (5%)
  other arithmetic  8.45 us (5%)
    ppermute x22, starting transfers between devices, shift(): lax.ppermute(value, axis, [(i, (i + step) % size) for i in range(size)])  75.2 us
    all_to_all x1, waiting for transfers between devices, on_device(): lax.all_to_all(jnp.stack([unembed] * lax.axis_size(('z', 'x'))), ('z', 'x...  25.8 us
    ppermute x22, waiting for transfers between devices, shift(): lax.ppermute(value, axis, [(i, (i + step) % size) for i in range(size)])  19.3 us
    all_to_all x1, starting transfers between devices, on_device(): lax.all_to_all(jnp.stack([unembed] * lax.axis_size(('z', 'x'))), ('z', 'x...  13.3 us
    unnamed x21, local copies, waits for them, and re-layouts  11.7 us
    dot_general x4, matrix products, chunk_stats(): lax.dot_general(normed, piece, (((1,), (1,)), ((), ())), preferred_elemen...  8.53 us
    reduce_sum x1, other arithmetic, chunk_stats(): jnp.sum(weights, axis=1)  3.86 us
    reshape x1, local copies, waits for them, and re-layouts, on_device(): jnp.concatenate(lax.all_to_all(jnp.stack([unembed] * lax.axis_size(('z',...  3.59 us
  transfers between devices with their start and end apart: 23, of which 6 were waited for; matrix products, arithmetic and copies ran while one was open for 14% of the time, Pallas kernels for 0%

profile of v1, /device:TPU:56, one launch (start us, length us, event | category | flops | bytes accessed | tf_op | source)
XLA Modules:
  0.0 171.9 jit_solution(12324356503250392202)
XLA Ops:
  0.6 2.9 %stack.4 = bf16[32,32,1600]{2,1,0:T(8,128)(2,1)} broadcast(bf16[32,1600]{1,0:T(8,128)(2,1)} %param.7), dimensions={1,2} | broadcast | bytes 3379200 | tf_op jit(solution)/shard_map/stack | solution.py:60
  3.5 13.3 %all-to-all-start = ((bf16[32,32,1600]{2,1,0:T(8,128)(2,1)}), bf16[32,32,1600]{2,1,0:T(8,128)(2,1)S(1)}, u32[]{:S(2)}, u32[]{:S(2)}) async-start(bf16[32,32,1600]{2,1,0:T(8,128)(2,1)} %stack.4), calls=%async_computation | async-start | bytes 6815744 | tf_op jit(solution)/shard_map/all_to_all | solution.py:60
  16.8 1.2 fusion.8
  18.0 2.2 %constant_dynamic-update-slice_fusion.8 = (bf16[1024,1600]{0,1:T(8,128)(2,1)}, bf16[128,1600]{0,1:T(8,128)(2,1)}) fusion(f32[1600]{0:T(1024)S(1)} %copy-done.1, f32[128]{0:T(128)S(1)} %add_rsqrt_fusion, bf16[128,1600]{0,1:T(8,128)(2,1)} %param.5), kind=kLoop, calls=%fused_computation.33 | loop fusion | flops 819199 | bytes 1235712
  20.2 3.2 %collective-permute-start.7 = (bf16[128,1600]{0,1:T(8,128)(2,1)}, bf16[128,1600]{0,1:T(8,128)(2,1)}, u32[]{:S(2)}, u32[]{:S(2)}) collective-permute-start(bf16[128,1600]{0,1:T(8,128)(2,1)} %get-tuple-element.18), channel_id=1, source_target_pairs={{0,7},{1,0},{2,1},{3,2},{4,3},{5,4},{6,5},{7,6},{8,15},{9,8},{10,9... | collective-permute-start | bytes 1228808 | tf_op jit(solution)/shard_map/ppermute | solution.py:21
  23.5 3.8 %collective-permute-start.10 = (bf16[128,1600]{0,1:T(8,128)(2,1)}, bf16[128,1600]{0,1:T(8,128)(2,1)}, u32[]{:S(2)}, u32[]{:S(2)}) collective-permute-start(bf16[128,1600]{0,1:T(8,128)(2,1)} %get-tuple-element.18), channel_id=1, source_target_pairs={{0,1},{1,2},{2,3},{3,4},{4,5},{5,6},{6,7},{7,0},{8,9},{9,10},{10,1... | collective-permute-start | bytes 1228808 | tf_op jit(solution)/shard_map/ppermute | solution.py:21
  27.3 2.0 %collective-permute-start = (s32[128]{0:T(128)S(1)}, s32[128]{0:T(128)S(1)}, u32[]{:S(2)}, u32[]{:S(2)}) collective-permute-start(s32[128]{0:T(128)S(1)} %copy-done.3), channel_id=1, source_target_pairs={{0,7},{1,0},{2,1},{3,2},{4,3},{5,4},{6,5},{7,6},{8,15},{9,8},{10,9... | collective-permute-start | bytes 1544 | tf_op jit(solution)/shard_map/ppermute | solution.py:21
  29.4 5.0 %collective-permute-start.3 = (s32[128]{0:T(128)S(1)}, s32[128]{0:T(128)S(1)}, u32[]{:S(2)}, u32[]{:S(2)}) collective-permute-start(s32[128]{0:T(128)S(1)} %copy-done.3), channel_id=1, source_target_pairs={{0,1},{1,2},{2,3},{3,4},{4,5},{5,6},{6,7},{7,0},{8,9},{9,10},{10,1... | collective-permute-start | bytes 1544 | tf_op jit(solution)/shard_map/ppermute | solution.py:21
  34.5 0.1 collective-permute-done
  34.6 2.0 %collective-permute-start.1 = (s32[128]{0:T(128)S(1)}, s32[128]{0:T(128)S(1)}, u32[]{:S(2)}, u32[]{:S(2)}) collective-permute-start(s32[128]{0:T(128)S(1)} %collective-permute-done), channel_id=1, source_target_pairs={{0,7},{1,0},{2,1},{3,2},{4,3},{5,4},{6,5},{7,6},{8,15},{9,8},{10,9... | collective-permute-start | bytes 1544 | tf_op jit(solution)/shard_map/ppermute | solution.py:21
  36.6 0.0 collective-permute-done.3
  36.6 5.0 %collective-permute-start.4 = (s32[128]{0:T(128)S(1)}, s32[128]{0:T(128)S(1)}, u32[]{:S(2)}, u32[]{:S(2)}) collective-permute-start(s32[128]{0:T(128)S(1)} %collective-permute-done.3), channel_id=1, source_target_pairs={{0,1},{1,2},{2,3},{3,4},{4,5},{5,6},{6,7},{7,0},{8,9},{9,10},{10,1... | collective-permute-start | bytes 1544 | tf_op jit(solution)/shard_map/ppermute | solution.py:21
  41.7 0.0 collective-permute-done.1
  41.7 1.9 %collective-permute-start.2 = (s32[128]{0:T(128)S(1)}, s32[128]{0:T(128)S(1)}, u32[]{:S(2)}, u32[]{:S(2)}) collective-permute-start(s32[128]{0:T(128)S(1)} %collective-permute-done.1), channel_id=1, source_target_pairs={{0,7},{1,0},{2,1},{3,2},{4,3},{5,4},{6,5},{7,6},{8,15},{9,8},{10,9... | collective-permute-start | bytes 1544 | tf_op jit(solution)/shard_map/ppermute | solution.py:21
  43.6 0.0 collective-permute-done.4
  43.6 5.1 %collective-permute-start.5 = (s32[128]{0:T(128)S(1)}, s32[128]{0:T(128)S(1)}, u32[]{:S(2)}, u32[]{:S(2)}) collective-permute-start(s32[128]{0:T(128)S(1)} %collective-permute-done.4), channel_id=1, source_target_pairs={{0,1},{1,2},{2,3},{3,4},{4,5},{5,6},{6,7},{7,0},{8,9},{9,10},{10,1... | collective-permute-start | bytes 1544 | tf_op jit(solution)/shard_map/ppermute | solution.py:21
  48.7 0.0 collective-permute-done.10
  48.8 1.9 %collective-permute-start.11 = (bf16[128,1600]{0,1:T(8,128)(2,1)}, bf16[128,1600]{0,1:T(8,128)(2,1)}, u32[]{:S(2)}, u32[]{:S(2)}) collective-permute-start(bf16[128,1600]{0,1:T(8,128)(2,1)} %collective-permute-done.10), channel_id=1, source_target_pairs={{0,1},{1,2},{2,3},{3,4},{4,5},{5,6},{6,7},{7,0},{8,9},{9,10},{10,1... | collective-permute-start | bytes 1228808 | tf_op jit(solution)/shard_map/ppermute | solution.py:21
  50.7 0.0 collective-permute-done.5
  50.7 4.7 %collective-permute-start.6 = (s32[128]{0:T(128)S(1)}, s32[128]{0:T(128)S(1)}, u32[]{:S(2)}, u32[]{:S(2)}) collective-permute-start(s32[128]{0:T(128)S(1)} %collective-permute-done.5), channel_id=1, source_target_pairs={{0,1},{1,2},{2,3},{3,4},{4,5},{5,6},{6,7},{7,0},{8,9},{9,10},{10,1... | collective-permute-start | bytes 1544 | tf_op jit(solution)/shard_map/ppermute | solution.py:21
  55.4 0.0 collective-permute-done.2
  55.4 0.0 collective-permute-done.7
  55.4 1.9 %collective-permute-start.8 = (bf16[128,1600]{0,1:T(8,128)(2,1)}, bf16[128,1600]{0,1:T(8,128)(2,1)}, u32[]{:S(2)}, u32[]{:S(2)}) collective-permute-start(bf16[128,1600]{0,1:T(8,128)(2,1)} %collective-permute-done.7), channel_id=1, source_target_pairs={{0,7},{1,0},{2,1},{3,2},{4,3},{5,4},{6,5},{7,6},{8,15},{9,8},{10,9... | collective-permute-start | bytes 1228808 | tf_op jit(solution)/shard_map/ppermute | solution.py:21
  57.3 2.5 %collective-permute-done.6 = s32[128]{0:T(128)S(1)} collective-permute-done((s32[128]{0:T(128)S(1)}, s32[128]{0:T(128)S(1)}, u32[]{:S(2)}, u32[]{:S(2)}) %collective-permute-start.6) | collective-permute-done | bytes 544 | tf_op jit(solution)/shard_map/ppermute | solution.py:21
  59.9 0.0 collective-permute-done.11
  59.9 3.4 %collective-permute-start.12 = (bf16[128,1600]{0,1:T(8,128)(2,1)}, bf16[128,1600]{0,1:T(8,128)(2,1)}, u32[]{:S(2)}, u32[]{:S(2)}) collective-permute-start(bf16[128,1600]{0,1:T(8,128)(2,1)} %collective-permute-done.11), channel_id=1, source_target_pairs={{0,1},{1,2},{2,3},{3,4},{4,5},{5,6},{6,7},{7,0},{8,9},{9,10},{10,1... | collective-permute-start | bytes 1228808 | tf_op jit(solution)/shard_map/ppermute | solution.py:21
  63.3 3.5 %collective-permute-done.8 = bf16[128,1600]{0,1:T(8,128)(2,1)} collective-permute-done((bf16[128,1600]{0,1:T(8,128)(2,1)}, bf16[128,1600]{0,1:T(8,128)(2,1)}, u32[]{:S(2)}, u32[]{:S(2)}) %collective-permute-start.8) | collective-permute-done | bytes 409632 | tf_op jit(solution)/shard_map/ppermute | solution.py:21
  66.9 1.9 %collective-permute-start.9 = (bf16[128,1600]{0,1:T(8,128)(2,1)}, bf16[128,1600]{0,1:T(8,128)(2,1)}, u32[]{:S(2)}, u32[]{:S(2)}) collective-permute-start(bf16[128,1600]{0,1:T(8,128)(2,1)} %collective-permute-done.8), channel_id=1, source_target_pairs={{0,7},{1,0},{2,1},{3,2},{4,3},{5,4},{6,5},{7,6},{8,15},{9,8},{10,9... | collective-permute-start | bytes 1228808 | tf_op jit(solution)/shard_map/ppermute | solution.py:21
  68.8 25.8 %all-to-all-done = bf16[32,32,1600]{2,1,0:T(8,128)(2,1)S(1)} async-done(((bf16[32,32,1600]{2,1,0:T(8,128)(2,1)}), bf16[32,32,1600]{2,1,0:T(8,128)(2,1)S(1)}, u32[]{:S(2)}, u32[]{:S(2)}) %all-to-all-start) | async-done | bytes 3276832 | tf_op jit(solution)/shard_map/all_to_all | solution.py:60
  94.6 3.6 %copy.9 = bf16[1024,1600]{0,1:T(8,128)(2,1)} copy(bf16[1024,1600]{1,0:T(8,128)(2,1)S(1)} %bitcast.596) | data formatting | bytes 6553600 | tf_op jit(solution)/shard_map/reshape | solution.py:59
  98.2 1.9 %collective-permute-start.14 = (bf16[1024,1600]{0,1:T(8,128)(2,1)}, bf16[1024,1600]{0,1:T(8,128)(2,1)S(1)}, u32[]{:S(2)}, u32[]{:S(2)}) collective-permute-start(bf16[1024,1600]{0,1:T(8,128)(2,1)} %copy.9), channel_id=1, source_target_pairs={{0,8},{8,0},{1,9},{9,1},{2,10},{10,2},{3,11},{11,3},{4,12},{12,4},... | collective-permute-start | bytes 9830408 | tf_op jit(solution)/shard_map/ppermute | solution.py:21
  100.1 1.8 %constant_dynamic-update-slice_fusion.7 = bf16[1024,1600]{0,1:T(8,128)(2,1)} fusion(bf16[1024,1600]{0,1:T(8,128)(2,1)} %get-tuple-element.17, bf16[128,1600]{0,1:T(8,128)(2,1)} %collective-permute-done.7), kind=kLoop, calls=%fused_computation.32 | loop fusion | bytes 819200
  102.0 0.0 collective-permute-done.12
  102.0 1.9 %collective-permute-start.13 = (bf16[128,1600]{0,1:T(8,128)(2,1)}, bf16[128,1600]{0,1:T(8,128)(2,1)S(1)}, u32[]{:S(2)}, u32[]{:S(2)}) collective-permute-start(bf16[128,1600]{0,1:T(8,128)(2,1)} %collective-permute-done.12), channel_id=1, source_target_pairs={{0,1},{1,2},{2,3},{3,4},{4,5},{5,6},{6,7},{7,0},{8,9},{9,10},{10,1... | collective-permute-start | bytes 1228808 | tf_op jit(solution)/shard_map/ppermute | solution.py:21
  103.9 1.8 %constant_dynamic-update-slice_fusion.6 = bf16[1024,1600]{0,1:T(8,128)(2,1)} fusion(bf16[1024,1600]{0,1:T(8,128)(2,1)} %constant_dynamic-update-slice_fusion.7, bf16[128,1600]{0,1:T(8,128)(2,1)} %collective-permute-done.8), kind=kLoop, calls=%fused_computation.31 | loop fusion | bytes 819200
  105.7 0.0 collective-permute-done.9
  105.7 1.8 %constant_dynamic-update-slice_fusion.5 = bf16[1024,1600]{0,1:T(8,128)(2,1)} fusion(bf16[1024,1600]{0,1:T(8,128)(2,1)} %constant_dynamic-update-slice_fusion.6, bf16[128,1600]{0,1:T(8,128)(2,1)} %collective-permute-done.9), kind=kLoop, calls=%fused_computation.30 | loop fusion | bytes 819200
  107.5 8.4 %collective-permute-done.13 = bf16[128,1600]{0,1:T(8,128)(2,1)S(1)} collective-permute-done((bf16[128,1600]{0,1:T(8,128)(2,1)}, bf16[128,1600]{0,1:T(8,128)(2,1)S(1)}, u32[]{:S(2)}, u32[]{:S(2)}) %collective-permute-start.13) | collective-permute-done | bytes 409632 | tf_op jit(solution)/shard_map/ppermute | solution.py:21
  115.9 0.8 constant_dynamic-update-slice_fusion.4
  116.7 1.8 %constant_dynamic-update-slice_fusion.3 = bf16[1024,1600]{0,1:T(8,128)(2,1)} fusion(bf16[1024,1600]{0,1:T(8,128)(2,1)} %constant_dynamic-update-slice_fusion.4, bf16[128,1600]{0,1:T(8,128)(2,1)} %collective-permute-done.12), kind=kLoop, calls=%fused_computation.28 | loop fusion | bytes 819200
  118.6 1.8 %constant_dynamic-update-slice_fusion.2 = bf16[1024,1600]{0,1:T(8,128)(2,1)} fusion(bf16[1024,1600]{0,1:T(8,128)(2,1)} %constant_dynamic-update-slice_fusion.3, bf16[128,1600]{0,1:T(8,128)(2,1)} %collective-permute-done.11), kind=kLoop, calls=%fused_computation.27 | loop fusion | bytes 819200
  120.4 1.8 %constant_dynamic-update-slice_fusion.1 = bf16[1024,1600]{0,1:T(8,128)(2,1)} fusion(bf16[1024,1600]{0,1:T(8,128)(2,1)} %constant_dynamic-update-slice_fusion.2, bf16[128,1600]{0,1:T(8,128)(2,1)} %collective-permute-done.10), kind=kLoop, calls=%fused_computation.26 | loop fusion | bytes 819200 | tf_op jit(solution)/shard_map/concatenate | solution.py:57
  122.2 0.3 fusion.81
  122.5 1.6 copy-done
  124.1 2.1 %fusion.87 = (f32[1024]{0:T(1024)S(1)}, f32[1024,512]{0,1:T(8,128)S(1)}) fusion(bf16[512,1600]{1,0:T(8,128)(2,1)S(1)} %bitcast.598, bf16[1024,1600]{0,1:T(8,128)(2,1)S(1)} %copy-done), kind=kOutput, calls=%fused_computation.198 | convolution fusion | flops 1678244864 | bytes 7016448 | tf_op jit(solution)/shard_map/dot_general | solution.py:25
  126.2 2.1 %fusion.84 = (f32[1024]{0:T(1024)S(1)}, f32[1024,512]{0,1:T(8,128)S(1)}) fusion(bf16[512,1600]{1,0:T(8,128)(2,1)S(1)} %bitcast.597, bf16[1024,1600]{0,1:T(8,128)(2,1)S(1)} %copy-done), kind=kOutput, calls=%fused_computation.195 | convolution fusion | flops 1678244864 | bytes 7016448 | tf_op jit(solution)/shard_map/dot_general | solution.py:25
  128.4 0.0 collective-permute-done.14
  128.4 2.1 %fusion.86 = (f32[1024]{0:T(1024)S(1)}, f32[1024,512]{0,1:T(8,128)S(1)}) fusion(bf16[1024,1600]{0,1:T(8,128)(2,1)S(1)} %copy-done, bf16[1024,1600]{0,1:T(8,128)(2,1)S(1)} %collective-permute-done.14), kind=kOutput, calls=%fused_computation.197 | convolution fusion | flops 1678244864 | bytes 7016448 | tf_op jit(solution)/shard_map/dot_general | solution.py:25
  130.5 2.1 %fusion.85 = (f32[1024]{0:T(1024)S(1)}, f32[1024,512]{0,1:T(8,128)S(1)}) fusion(bf16[1024,1600]{0,1:T(8,128)(2,1)S(1)} %copy-done, bf16[1024,1600]{0,1:T(8,128)(2,1)S(1)} %collective-permute-done.14), kind=kOutput, calls=%fused_computation.196 | convolution fusion | flops 1678244864 | bytes 7016448 | tf_op jit(solution)/shard_map/dot_general | solution.py:25
  132.7 0.0 copy-start.2
  132.7 3.9 %exponential_reduce_fusion.2 = (f32[1024]{0:T(1024)S(1)}, f32[1024]{0:T(1024)S(1)}, f32[1024]{0:T(1024)S(1)}, f32[1024]{0:T(1024)S(1)}, f32[1024]{0:T(1024)S(1)}...) fusion(f32[1024,512]{0,1:T(8,128)S(1)} %get-tuple-element.45, ...), kind=kLoop, calls=%fused_computation.5 | loop fusion | flops 14667776 | bytes 8466432 | tf_op jit(solution)/shard_map/reduce_sum | solution.py:32
  136.6 3.4 %collective-permute-start.15 = (f32[4,128]{1,0:T(4,128)S(1)}, f32[4,128]{1,0:T(4,128)S(1)}, u32[]{:S(2)}, u32[]{:S(2)}) collective-permute-start(f32[4,128]{1,0:T(4,128)S(1)} %bitcast.602), channel_id=1, source_target_pairs={{0,1},{1,2},{2,3},{3,4},{4,5},{5,6},{6,7},{7,0},{8,9},{9,10},{10,1... | collective-permute-start | bytes 6152 | tf_op jit(solution)/shard_map/ppermute | solution.py:21
  140.1 7.2 %collective-permute-start.18 = (f32[4,128]{1,0:T(4,128)S(1)}, f32[4,128]{1,0:T(4,128)S(1)}, u32[]{:S(2)}, u32[]{:S(2)}) collective-permute-start(f32[4,128]{1,0:T(4,128)S(1)} %bitcast.601), channel_id=1, source_target_pairs={{0,4},{1,5},{2,6},{3,7},{4,0},{5,1},{6,2},{7,3},{8,12},{9,13},{10,... | collective-permute-start | bytes 6152 | tf_op jit(solution)/shard_map/ppermute | solution.py:21
  147.3 1.9 %collective-permute-start.19 = (f32[4,128]{1,0:T(4,128)S(1)}, f32[4,128]{1,0:T(4,128)S(1)}, u32[]{:S(2)}, u32[]{:S(2)}) collective-permute-start(f32[4,128]{1,0:T(4,128)S(1)} %bitcast.600), channel_id=1, source_target_pairs={{0,5},{1,6},{2,7},{3,0},{4,1},{5,2},{6,3},{7,4},{8,13},{9,14},{10,... | collective-permute-start | bytes 6152 | tf_op jit(solution)/shard_map/ppermute | solution.py:21
  149.2 3.1 %collective-permute-start.20 = (f32[4,128]{1,0:T(4,128)S(1)}, f32[4,128]{1,0:T(4,128)S(1)}, u32[]{:S(2)}, u32[]{:S(2)}) collective-permute-start(f32[4,128]{1,0:T(4,128)S(1)} %bitcast.599), channel_id=1, source_target_pairs={{0,6},{1,7},{2,0},{3,1},{4,2},{5,3},{6,4},{7,5},{8,14},{9,15},{10,... | collective-permute-start | bytes 6152 | tf_op jit(solution)/shard_map/ppermute | solution.py:21
  152.3 4.9 %collective-permute-start.16 = (f32[4,128]{1,0:T(4,128)S(1)}, f32[4,128]{1,0:T(4,128)S(1)}, u32[]{:S(2)}, u32[]{:S(2)}) collective-permute-start(f32[4,128]{1,0:T(4,128)S(1)} %bitcast.605), channel_id=1, source_target_pairs={{0,2},{1,3},{2,4},{3,5},{4,6},{5,7},{6,0},{7,1},{8,10},{9,11},{10,... | collective-permute-start | bytes 6152 | tf_op jit(solution)/shard_map/ppermute | solution.py:21
  157.2 0.0 collective-permute-done.15
  157.2 6.9 %collective-permute-start.17 = (f32[4,128]{1,0:T(4,128)S(1)}, f32[4,128]{1,0:T(4,128)S(1)}, u32[]{:S(2)}, u32[]{:S(2)}) collective-permute-start(f32[4,128]{1,0:T(4,128)S(1)} %bitcast.604), channel_id=1, source_target_pairs={{0,3},{1,4},{2,5},{3,6},{4,7},{5,0},{6,1},{7,2},{8,11},{9,12},{10,... | collective-permute-start | bytes 6152 | tf_op jit(solution)/shard_map/ppermute | solution.py:21
  164.1 1.9 %collective-permute-start.21 = (f32[4,128]{1,0:T(4,128)S(1)}, f32[4,128]{1,0:T(4,128)S(1)}, u32[]{:S(2)}, u32[]{:S(2)}) collective-permute-start(f32[4,128]{1,0:T(4,128)S(1)} %bitcast.603), channel_id=1, source_target_pairs={{0,7},{1,0},{2,1},{3,2},{4,3},{5,4},{6,5},{7,6},{8,15},{9,8},{10,9... | collective-permute-start | bytes 6152 | tf_op jit(solution)/shard_map/ppermute | solution.py:21
  166.1 0.0 collective-permute-done.19
  166.1 0.0 collective-permute-done.17
  166.1 4.7 %collective-permute-done.21 = f32[4,128]{1,0:T(4,128)S(1)} collective-permute-done((f32[4,128]{1,0:T(4,128)S(1)}, f32[4,128]{1,0:T(4,128)S(1)}, u32[]{:S(2)}, u32[]{:S(2)}) %collective-permute-start.21) | collective-permute-done | bytes 2080 | tf_op jit(solution)/shard_map/ppermute | solution.py:21
  170.8 0.5 subtract_multiply_fusion
  171.4 0.5 fusion.78
  (26 shorter events, 0.2 us)
Async XLA Ops:
  3.5 14.5 %copy-start.1 = (f32[1600]{0:T(1024)S(1)}, f32[1600]{0:T(1024)}, u32[]{:S(2)}) copy-start(f32[1600]{0:T(1024)} %param.6) | copy-start | bytes 19204
  3.5 23.8 %copy-start.3 = (s32[128]{0:T(128)S(1)}, s32[128]{0:T(128)}, u32[]{:S(2)}) copy-start(s32[128]{0:T(128)} %param.8) | copy-start | bytes 1540
  3.5 91.1 %all-to-all-start = ((bf16[32,32,1600]{2,1,0:T(8,128)(2,1)}), bf16[32,32,1600]{2,1,0:T(8,128)(2,1)S(1)}, u32[]{:S(2)}, u32[]{:S(2)}) async-start(bf16[32,32,1600]{2,1,0:T(8,128)(2,1)} %stack.4), calls=%async_computation | async-start | bytes 6815744 | tf_op jit(solution)/shard_map/all_to_all | solution.py:60
  20.2 35.2 %collective-permute-start.7 = (bf16[128,1600]{0,1:T(8,128)(2,1)}, bf16[128,1600]{0,1:T(8,128)(2,1)}, u32[]{:S(2)}, u32[]{:S(2)}) collective-permute-start(bf16[128,1600]{0,1:T(8,128)(2,1)} %get-tuple-element.18), channel_id=1, source_target_pairs={{0,7},{1,0},{2,1},{3,2},{4,3},{5,4},{6,5},{7,6},{8,15},{9,8},{10,9... | collective-permute-start | bytes 1228808 | tf_op jit(solution)/shard_map/ppermute | solution.py:21
  23.5 25.3 %collective-permute-start.10 = (bf16[128,1600]{0,1:T(8,128)(2,1)}, bf16[128,1600]{0,1:T(8,128)(2,1)}, u32[]{:S(2)}, u32[]{:S(2)}) collective-permute-start(bf16[128,1600]{0,1:T(8,128)(2,1)} %get-tuple-element.18), channel_id=1, source_target_pairs={{0,1},{1,2},{2,3},{3,4},{4,5},{5,6},{6,7},{7,0},{8,9},{9,10},{10,1... | collective-permute-start | bytes 1228808 | tf_op jit(solution)/shard_map/ppermute | solution.py:21
  27.3 7.3 %collective-permute-start = (s32[128]{0:T(128)S(1)}, s32[128]{0:T(128)S(1)}, u32[]{:S(2)}, u32[]{:S(2)}) collective-permute-start(s32[128]{0:T(128)S(1)} %copy-done.3), channel_id=1, source_target_pairs={{0,7},{1,0},{2,1},{3,2},{4,3},{5,4},{6,5},{7,6},{8,15},{9,8},{10,9... | collective-permute-start | bytes 1544 | tf_op jit(solution)/shard_map/ppermute | solution.py:21
  29.4 7.3 %collective-permute-start.3 = (s32[128]{0:T(128)S(1)}, s32[128]{0:T(128)S(1)}, u32[]{:S(2)}, u32[]{:S(2)}) collective-permute-start(s32[128]{0:T(128)S(1)} %copy-done.3), channel_id=1, source_target_pairs={{0,1},{1,2},{2,3},{3,4},{4,5},{5,6},{6,7},{7,0},{8,9},{9,10},{10,1... | collective-permute-start | bytes 1544 | tf_op jit(solution)/shard_map/ppermute | solution.py:21
  34.6 7.1 %collective-permute-start.1 = (s32[128]{0:T(128)S(1)}, s32[128]{0:T(128)S(1)}, u32[]{:S(2)}, u32[]{:S(2)}) collective-permute-start(s32[128]{0:T(128)S(1)} %collective-permute-done), channel_id=1, source_target_pairs={{0,7},{1,0},{2,1},{3,2},{4,3},{5,4},{6,5},{7,6},{8,15},{9,8},{10,9... | collective-permute-start | bytes 1544 | tf_op jit(solution)/shard_map/ppermute | solution.py:21
  36.6 7.0 %collective-permute-start.4 = (s32[128]{0:T(128)S(1)}, s32[128]{0:T(128)S(1)}, u32[]{:S(2)}, u32[]{:S(2)}) collective-permute-start(s32[128]{0:T(128)S(1)} %collective-permute-done.3), channel_id=1, source_target_pairs={{0,1},{1,2},{2,3},{3,4},{4,5},{5,6},{6,7},{7,0},{8,9},{9,10},{10,1... | collective-permute-start | bytes 1544 | tf_op jit(solution)/shard_map/ppermute | solution.py:21
  41.7 13.7 %collective-permute-start.2 = (s32[128]{0:T(128)S(1)}, s32[128]{0:T(128)S(1)}, u32[]{:S(2)}, u32[]{:S(2)}) collective-permute-start(s32[128]{0:T(128)S(1)} %collective-permute-done.1), channel_id=1, source_target_pairs={{0,7},{1,0},{2,1},{3,2},{4,3},{5,4},{6,5},{7,6},{8,15},{9,8},{10,9... | collective-permute-start | bytes 1544 | tf_op jit(solution)/shard_map/ppermute | solution.py:21
  43.6 7.1 %collective-permute-start.5 = (s32[128]{0:T(128)S(1)}, s32[128]{0:T(128)S(1)}, u32[]{:S(2)}, u32[]{:S(2)}) collective-permute-start(s32[128]{0:T(128)S(1)} %collective-permute-done.4), channel_id=1, source_target_pairs={{0,1},{1,2},{2,3},{3,4},{4,5},{5,6},{6,7},{7,0},{8,9},{9,10},{10,1... | collective-permute-start | bytes 1544 | tf_op jit(solution)/shard_map/ppermute | solution.py:21
  48.8 11.1 %collective-permute-start.11 = (bf16[128,1600]{0,1:T(8,128)(2,1)}, bf16[128,1600]{0,1:T(8,128)(2,1)}, u32[]{:S(2)}, u32[]{:S(2)}) collective-permute-start(bf16[128,1600]{0,1:T(8,128)(2,1)} %collective-permute-done.10), channel_id=1, source_target_pairs={{0,1},{1,2},{2,3},{3,4},{4,5},{5,6},{6,7},{7,0},{8,9},{9,10},{10,1... | collective-permute-start | bytes 1228808 | tf_op jit(solution)/shard_map/ppermute | solution.py:21
  50.7 9.2 %collective-permute-start.6 = (s32[128]{0:T(128)S(1)}, s32[128]{0:T(128)S(1)}, u32[]{:S(2)}, u32[]{:S(2)}) collective-permute-start(s32[128]{0:T(128)S(1)} %collective-permute-done.5), channel_id=1, source_target_pairs={{0,1},{1,2},{2,3},{3,4},{4,5},{5,6},{6,7},{7,0},{8,9},{9,10},{10,1... | collective-permute-start | bytes 1544 | tf_op jit(solution)/shard_map/ppermute | solution.py:21
  55.4 11.5 %collective-permute-start.8 = (bf16[128,1600]{0,1:T(8,128)(2,1)}, bf16[128,1600]{0,1:T(8,128)(2,1)}, u32[]{:S(2)}, u32[]{:S(2)}) collective-permute-start(bf16[128,1600]{0,1:T(8,128)(2,1)} %collective-permute-done.7), channel_id=1, source_target_pairs={{0,7},{1,0},{2,1},{3,2},{4,3},{5,4},{6,5},{7,6},{8,15},{9,8},{10,9... | collective-permute-start | bytes 1228808 | tf_op jit(solution)/shard_map/ppermute | solution.py:21
  59.9 42.1 %collective-permute-start.12 = (bf16[128,1600]{0,1:T(8,128)(2,1)}, bf16[128,1600]{0,1:T(8,128)(2,1)}, u32[]{:S(2)}, u32[]{:S(2)}) collective-permute-start(bf16[128,1600]{0,1:T(8,128)(2,1)} %collective-permute-done.11), channel_id=1, source_target_pairs={{0,1},{1,2},{2,3},{3,4},{4,5},{5,6},{6,7},{7,0},{8,9},{9,10},{10,1... | collective-permute-start | bytes 1228808 | tf_op jit(solution)/shard_map/ppermute | solution.py:21
  66.9 38.8 %collective-permute-start.9 = (bf16[128,1600]{0,1:T(8,128)(2,1)}, bf16[128,1600]{0,1:T(8,128)(2,1)}, u32[]{:S(2)}, u32[]{:S(2)}) collective-permute-start(bf16[128,1600]{0,1:T(8,128)(2,1)} %collective-permute-done.8), channel_id=1, source_target_pairs={{0,7},{1,0},{2,1},{3,2},{4,3},{5,4},{6,5},{7,6},{8,15},{9,8},{10,9... | collective-permute-start | bytes 1228808 | tf_op jit(solution)/shard_map/ppermute | solution.py:21
  98.2 30.2 %collective-permute-start.14 = (bf16[1024,1600]{0,1:T(8,128)(2,1)}, bf16[1024,1600]{0,1:T(8,128)(2,1)S(1)}, u32[]{:S(2)}, u32[]{:S(2)}) collective-permute-start(bf16[1024,1600]{0,1:T(8,128)(2,1)} %copy.9), channel_id=1, source_target_pairs={{0,8},{8,0},{1,9},{9,1},{2,10},{10,2},{3,11},{11,3},{4,12},{12,4},... | collective-permute-start | bytes 9830408 | tf_op jit(solution)/shard_map/ppermute | solution.py:21
  102.0 14.0 %collective-permute-start.13 = (bf16[128,1600]{0,1:T(8,128)(2,1)}, bf16[128,1600]{0,1:T(8,128)(2,1)S(1)}, u32[]{:S(2)}, u32[]{:S(2)}) collective-permute-start(bf16[128,1600]{0,1:T(8,128)(2,1)} %collective-permute-done.12), channel_id=1, source_target_pairs={{0,1},{1,2},{2,3},{3,4},{4,5},{5,6},{6,7},{7,0},{8,9},{9,10},{10,1... | collective-permute-start | bytes 1228808 | tf_op jit(solution)/shard_map/ppermute | solution.py:21
  122.2 1.9 %copy-start = (bf16[1024,1600]{0,1:T(8,128)(2,1)S(1)}, bf16[1024,1600]{0,1:T(8,128)(2,1)}, u32[]{:S(2)}) copy-start(bf16[1024,1600]{0,1:T(8,128)(2,1)} %constant_dynamic-update-slice_fusion.1) | copy-start | bytes 9830404
  132.7 38.1 %copy-start.2 = (s32[128]{0:T(128)S(1)}, s32[128]{0:T(128)}, u32[]{:S(2)}) copy-start(s32[128]{0:T(128)} %param.9) | copy-start | bytes 1540
  136.6 20.5 %collective-permute-start.15 = (f32[4,128]{1,0:T(4,128)S(1)}, f32[4,128]{1,0:T(4,128)S(1)}, u32[]{:S(2)}, u32[]{:S(2)}) collective-permute-start(f32[4,128]{1,0:T(4,128)S(1)} %bitcast.602), channel_id=1, source_target_pairs={{0,1},{1,2},{2,3},{3,4},{4,5},{5,6},{6,7},{7,0},{8,9},{9,10},{10,1... | collective-permute-start | bytes 6152 | tf_op jit(solution)/shard_map/ppermute | solution.py:21
  140.1 24.1 %collective-permute-start.18 = (f32[4,128]{1,0:T(4,128)S(1)}, f32[4,128]{1,0:T(4,128)S(1)}, u32[]{:S(2)}, u32[]{:S(2)}) collective-permute-start(f32[4,128]{1,0:T(4,128)S(1)} %bitcast.601), channel_id=1, source_target_pairs={{0,4},{1,5},{2,6},{3,7},{4,0},{5,1},{6,2},{7,3},{8,12},{9,13},{10,... | collective-permute-start | bytes 6152 | tf_op jit(solution)/shard_map/ppermute | solution.py:21
  147.3 18.8 %collective-permute-start.19 = (f32[4,128]{1,0:T(4,128)S(1)}, f32[4,128]{1,0:T(4,128)S(1)}, u32[]{:S(2)}, u32[]{:S(2)}) collective-permute-start(f32[4,128]{1,0:T(4,128)S(1)} %bitcast.600), channel_id=1, source_target_pairs={{0,5},{1,6},{2,7},{3,0},{4,1},{5,2},{6,3},{7,4},{8,13},{9,14},{10,... | collective-permute-start | bytes 6152 | tf_op jit(solution)/shard_map/ppermute | solution.py:21
  149.2 16.9 %collective-permute-start.20 = (f32[4,128]{1,0:T(4,128)S(1)}, f32[4,128]{1,0:T(4,128)S(1)}, u32[]{:S(2)}, u32[]{:S(2)}) collective-permute-start(f32[4,128]{1,0:T(4,128)S(1)} %bitcast.599), channel_id=1, source_target_pairs={{0,6},{1,7},{2,0},{3,1},{4,2},{5,3},{6,4},{7,5},{8,14},{9,15},{10,... | collective-permute-start | bytes 6152 | tf_op jit(solution)/shard_map/ppermute | solution.py:21
  152.3 13.8 %collective-permute-start.16 = (f32[4,128]{1,0:T(4,128)S(1)}, f32[4,128]{1,0:T(4,128)S(1)}, u32[]{:S(2)}, u32[]{:S(2)}) collective-permute-start(f32[4,128]{1,0:T(4,128)S(1)} %bitcast.605), channel_id=1, source_target_pairs={{0,2},{1,3},{2,4},{3,5},{4,6},{5,7},{6,0},{7,1},{8,10},{9,11},{10,... | collective-permute-start | bytes 6152 | tf_op jit(solution)/shard_map/ppermute | solution.py:21
  157.2 8.9 %collective-permute-start.17 = (f32[4,128]{1,0:T(4,128)S(1)}, f32[4,128]{1,0:T(4,128)S(1)}, u32[]{:S(2)}, u32[]{:S(2)}) collective-permute-start(f32[4,128]{1,0:T(4,128)S(1)} %bitcast.604), channel_id=1, source_target_pairs={{0,3},{1,4},{2,5},{3,6},{4,7},{5,0},{6,1},{7,2},{8,11},{9,12},{10,... | collective-permute-start | bytes 6152 | tf_op jit(solution)/shard_map/ppermute | solution.py:21
  164.1 6.7 %collective-permute-start.21 = (f32[4,128]{1,0:T(4,128)S(1)}, f32[4,128]{1,0:T(4,128)S(1)}, u32[]{:S(2)}, u32[]{:S(2)}) collective-permute-start(f32[4,128]{1,0:T(4,128)S(1)} %bitcast.603), channel_id=1, source_target_pairs={{0,7},{1,0},{2,1},{3,2},{4,3},{5,4},{6,5},{7,6},{8,15},{9,8},{10,9... | collective-permute-start | bytes 6152 | tf_op jit(solution)/shard_map/ppermute | solution.py:21
